TPU v7x, 32 devices: a whole 2x2x4 slice. The times are simulated.
32 devices in a mesh: dp: 4 (over y, core), mp: 8 (over z, x).
Axes of the slice: x: 2, y: 2, z: 4, core: 2. Of those that a mesh axis runs over, the one named last changes fastest.
Arguments:
- tokens: bfloat16 [512, 6144], P('dp', 'mp'), may hold values from -6 to 6
- norm_gain: bfloat16 [6144], P('mp'), may hold values from 0.5 to 1.5
- qkv_weight: bfloat16 [3, 128, 24, 6144], P(None, 'mp', None, 'dp'), may hold values from -0.078125 to 0.078125
- head_weight: bfloat16 [128, 24, 6144], P('mp', None, 'dp'), may hold values from -0.109375 to 0.109375
- up_weight: bfloat16 [12288, 6144], P('mp', 'dp'), may hold values from -0.078125 to 0.078125
- down_weight: bfloat16 [12288, 6144], P('mp', 'dp'), may hold values from -0.0546875 to 0.0546875
- cotangent: bfloat16 [512, 6144], P('dp', 'mp'), may hold values from -6 to 6
Outputs:
- mixed: bfloat16 [512, 6144], P('dp', 'mp')
- tokens_grad: float32 [512, 6144], P('dp', 'mp')
- qkv_grad: bfloat16 [3, 128, 24, 6144], P(None, 'mp', None, 'dp')
- head_grad: bfloat16 [128, 24, 6144], P('mp', None, 'dp')
- up_grad: bfloat16 [12288, 6144], P('mp', 'dp')
- down_grad: bfloat16 [12288, 6144], P('mp', 'dp')
- gain_grad: float32 [6144], P('mp')
All inputs are finite; a program needn't handle non-finite values.
Results may differ from a plain program's by a relative error of at most 0.013.
Values may be sent and summed in bfloat16 or wider, within the bound.
No kernel may reach another device: no remote copies, remote signals or barrier semaphores. Data moves between devices by JAX's collectives and lax.ppermute only.
A program may use at most 256 MiB of HBM per device.

v0:
```python
import math

import jax
import jax.numpy as jnp
from jax import lax
from jax.sharding import PartitionSpec as P

D = 6144
HEADS = 24
HS = 128
PATCHES = 128
QB = 8
IMG_DP = 1
ROWS = 128
TQ = 16
ITEMS = 192


epsilon = 1e-06
contract_rows = (((0,), (0,)), ((), ()))
contract_cols = (((1,), (1,)), ((), ()))


def gelu_pair(inputs):
    normal_cdf = 0.5 * (1.0 + jax.scipy.special.erf(inputs * 0.7071067811865476))
    density = jnp.exp(-0.5 * inputs * inputs) * 0.3989422804014327
    return (inputs * normal_cdf, normal_cdf + inputs * density)


def head_norm(values):
    center = values - jnp.mean(values, axis=0, keepdims=True)
    inverse = lax.rsqrt(jnp.mean(center * center, axis=0, keepdims=True) + epsilon)
    return (center * inverse, inverse)


def norm_back(upstream, normed, inverse):
    return inverse * (
        upstream
        - jnp.mean(upstream, axis=0, keepdims=True)
        - normed * jnp.mean(upstream * normed, axis=0, keepdims=True)
    )


def to_items(pair_rows):
    depth = pair_rows.shape[1]
    shaped = pair_rows.reshape(2, depth, HEADS, IMG_DP, 1, PATCHES)
    spread = jnp.broadcast_to(shaped, (2, depth, HEADS, IMG_DP, QB, PATCHES))
    return jnp.transpose(spread, (1, 2, 3, 4, 0, 5)).reshape(depth, HEADS * IMG_DP * QB, 2, PATCHES)


def from_items(pair_items):
    depth = pair_items.shape[0]
    shaped = pair_items.reshape(depth, HEADS, IMG_DP, QB, 2, PATCHES)
    summed = jnp.sum(shaped.astype(jnp.float32), axis=3).astype(jnp.bfloat16)
    return jnp.transpose(summed, (3, 0, 1, 2, 4)).reshape(2, depth, HEADS, IMG_DP * PATCHES)


def attend(queries, keyvals):
    query_hat, query_scale = head_norm(queries.astype(jnp.float32))
    key_hat, key_scale = head_norm(keyvals[:, :, 0].astype(jnp.float32))
    query_norm = query_hat.astype(jnp.bfloat16)
    key_norm = key_hat.astype(jnp.bfloat16)
    factor = 1.0 / math.sqrt(queries.shape[0])
    scores = (
        jnp.einsum("cia,cib->iab", query_norm, key_norm, preferred_element_type=jnp.float32)
        * factor
    )
    raised = jnp.exp(scores)
    shares = raised / jnp.sum(raised, axis=2, keepdims=True)
    rounded = shares.astype(jnp.bfloat16)
    values = keyvals[:, :, 1]
    attended = jnp.einsum(
        "iab,cib->cia", rounded, values, preferred_element_type=jnp.float32
    ).astype(jnp.bfloat16)
    stored = (
        query_hat,
        query_scale,
        key_hat,
        key_scale,
        query_norm,
        key_norm,
        shares,
        rounded,
        values,
    )
    return (attended, stored)


def attend_back(upstream, stored):
    query_hat, query_scale, key_hat, key_scale, query_norm, key_norm, shares, rounded, values = (
        stored
    )
    factor = 1.0 / math.sqrt(upstream.shape[0])
    share_grad = jnp.einsum("cia,cib->iab", upstream, values, preferred_element_type=jnp.float32)
    value_grad = jnp.einsum("iab,cia->cib", rounded, upstream, preferred_element_type=jnp.float32)
    score_grad = (
        shares * (share_grad - jnp.sum(shares * share_grad, axis=2, keepdims=True)) * factor
    ).astype(jnp.bfloat16)
    query_back = jnp.einsum(
        "iab,cib->cia", score_grad, key_norm, preferred_element_type=jnp.float32
    )
    key_back = jnp.einsum(
        "iab,cia->cib", score_grad, query_norm, preferred_element_type=jnp.float32
    )
    query_grad = norm_back(query_back, query_hat, query_scale).astype(jnp.bfloat16)
    key_grad = norm_back(key_back, key_hat, key_scale).astype(jnp.bfloat16)
    pair_grad = jnp.stack([key_grad, value_grad.astype(jnp.bfloat16)], axis=2)
    return (query_grad, pair_grad)


def swap_pairs(n_dp, n_mp):
    ratio = n_mp // n_dp
    pairs = []
    for row in range(n_dp):
        for col in range(n_mp):
            owner, part = divmod(col, ratio)
            pairs.append((row * n_mp + col, owner * n_mp + row * ratio + part))
    return pairs


def swap_by_part_pairs(n_dp, n_mp):
    ratio = n_mp // n_dp
    pairs = []
    for row in range(n_dp):
        for col in range(n_mp):
            part, owner = divmod(col, n_dp)
            pairs.append((row * n_mp + col, owner * n_mp + row * ratio + part))
    return pairs


def swap(block):
    n_dp, n_mp = lax.axis_size("dp"), lax.axis_size("mp")
    return lax.ppermute(block, ("dp", "mp"), swap_pairs(n_dp, n_mp))


def spread_quarter(block):
    n_dp, n_mp = lax.axis_size("dp"), lax.axis_size("mp")
    ratio = n_mp // n_dp
    rows, width = block.shape
    copies = jnp.broadcast_to(swap(block)[None], (n_mp, rows, width))
    pieces = lax.all_to_all(copies, "mp", split_axis=0, concat_axis=0, tiled=True)
    pieces = pieces.reshape(n_dp, ratio, rows, width)
    return jnp.transpose(pieces, (0, 2, 1, 3)).reshape(n_dp * rows, ratio * width)


def spread_quarter_rows(block):
    n_dp, n_mp = lax.axis_size("dp"), lax.axis_size("mp")
    ratio = n_mp // n_dp
    rows, width = block.shape
    copies = jnp.broadcast_to(swap(block)[None], (n_mp, rows, width))
    pieces = lax.all_to_all(copies, "mp", split_axis=0, concat_axis=0, tiled=True)
    pieces = pieces.reshape(n_dp, ratio, rows, width)
    return jnp.transpose(pieces, (0, 2, 1, 3)).reshape(n_dp, rows, ratio * width)


def gather_quarter(partial, rows):
    n_dp, n_mp = lax.axis_size("dp"), lax.axis_size("mp")
    ratio = n_mp // n_dp
    width = partial.shape[1] // ratio
    pieces = partial.reshape(n_dp, rows, ratio, width)
    pieces = jnp.transpose(pieces, (0, 2, 1, 3)).reshape(n_mp, rows, width)
    summed = lax.psum_scatter(pieces, "mp", scatter_dimension=0, tiled=True)
    return swap(summed.reshape(rows, width))


def gather_quarter_exchange(partial, rows):
    n_dp, n_mp = lax.axis_size("dp"), lax.axis_size("mp")
    ratio = n_mp // n_dp
    width = partial.shape[1] // ratio
    pieces = partial.reshape(n_dp, rows, ratio, width)
    pieces = jnp.transpose(pieces, (0, 2, 1, 3)).reshape(n_mp, rows, width)
    received = lax.all_to_all(pieces, "mp", split_axis=0, concat_axis=0, tiled=True)
    return swap(jnp.sum(received, axis=0))


def blockwise_grad(left, right, n_blocks):
    rows = left.shape[1] // n_blocks
    total = None
    for block in range(n_blocks):
        piece = jnp.dot(
            left[:, block * rows:(block + 1) * rows],
            right[block * rows:(block + 1) * rows],
            preferred_element_type=jnp.float32,
        ).astype(jnp.bfloat16).astype(jnp.float32)
        total = piece if total is None else total + piece
    return total.astype(jnp.bfloat16)


def shards(tokens, norm_gain, qkv_weight, head_weight, up_weight, down_weight, cotangent):
    n_dp, n_mp = lax.axis_size("dp"), lax.axis_size("mp")
    head_slice = HS // n_mp
    quarter = qkv_weight.shape[-1]
    rows, width = tokens.shape
    qkv_flat = qkv_weight.reshape(-1, quarter)
    head_flat = head_weight.reshape(-1, quarter)

    widened = tokens.astype(jnp.float32)
    gain_wide = norm_gain.astype(jnp.float32)
    with_gain = jnp.concatenate([tokens, norm_gain.reshape(1, width)], axis=0)
    spread_in = spread_quarter_rows(with_gain)
    tokens_all = spread_in[:, :rows].reshape(-1, quarter).astype(jnp.float32)
    gain_quarter = spread_in[0, rows].astype(jnp.float32)
    part_mean = jnp.mean(tokens_all, axis=1)
    part_center = tokens_all - part_mean[:, None]
    part_m2 = jnp.sum(part_center * part_center, axis=1)
    parts = lax.all_gather(jnp.stack([part_mean, part_m2]), "dp", axis=0, tiled=False)
    mean_all = jnp.mean(parts[:, 0], axis=0)
    spread = parts[:, 0] - mean_all[None, :]
    m2_all = jnp.sum(parts[:, 1], axis=0) + quarter * jnp.sum(spread * spread, axis=0)
    scale_all = lax.rsqrt(m2_all / D + epsilon)
    hidden_all = (
        ((tokens_all - mean_all[:, None]) * scale_all[:, None]) * gain_quarter
    ).astype(jnp.bfloat16)
    me = lax.axis_index("dp")
    row_mean = lax.dynamic_slice_in_dim(mean_all, me * rows, rows)[:, None]
    row_scale = lax.dynamic_slice_in_dim(scale_all, me * rows, rows)[:, None]
    normed = (widened - row_mean) * row_scale
    cot_all = spread_quarter(cotangent)

    n_proj = qkv_flat.shape[0]
    proj_up = jnp.concatenate(
        [
            lax.dot_general(qkv_flat, hidden_all, contract_cols, preferred_element_type=jnp.float32),
            lax.dot_general(up_weight, hidden_all, contract_cols, preferred_element_type=jnp.float32),
        ],
        axis=0,
    )
    proj_up = lax.psum_scatter(proj_up, "dp", scatter_dimension=1, tiled=True)
    cot_later, proj_up = lax.optimization_barrier((cot_all, proj_up))
    projected = proj_up[:n_proj].astype(jnp.bfloat16).reshape(3, head_slice, HEADS, ROWS)
    up_input = proj_up[n_proj:]
    activated, gelu_slope = gelu_pair(up_input)
    up_output = activated.astype(jnp.bfloat16)

    by_head = HEADS % n_mp == 0
    if by_head:
        head_group = HEADS // n_mp
        qkv_heads = lax.all_to_all(projected, "mp", split_axis=2, concat_axis=1, tiled=True)
        query_heads = qkv_heads[0].reshape(HS, head_group * QB, TQ)
        pairs = jnp.stack([qkv_heads[1], qkv_heads[2]], axis=2)
        pair_heads = jnp.broadcast_to(
            pairs[:, :, None], (HS, head_group, QB, 2, PATCHES)
        ).reshape(HS, head_group * QB, 2, PATCHES)
        attended, stored = attend(query_heads, pair_heads)
        head_rows = lax.all_to_all(
            attended.reshape(HS, head_group, ROWS), "mp", split_axis=0, concat_axis=1, tiled=True
        ).reshape(head_slice * HEADS, ROWS)
    else:
        queries = projected[0].reshape(head_slice, ITEMS, TQ)
        keyvals = to_items(projected[1:])
        query_heads, pair_heads = (
            lax.all_to_all(queries, "mp", split_axis=1, concat_axis=0, tiled=True),
            lax.all_to_all(keyvals, "mp", split_axis=1, concat_axis=0, tiled=True),
        )
        attended, stored = attend(query_heads, pair_heads)
        head_rows = lax.all_to_all(attended, "mp", split_axis=0, concat_axis=1, tiled=True).reshape(
            head_slice * HEADS, ROWS
        )
    n_att = head_rows.shape[0]
    both_all = lax.all_gather(
        jnp.concatenate([head_rows, up_output], axis=0), "dp", axis=1, tiled=True
    )
    head_rows_all, up_output_all = both_all[:n_att], both_all[n_att:]
    branch = lax.dot_general(
        head_rows_all, head_flat, contract_rows, preferred_element_type=jnp.float32
    ) + lax.dot_general(up_output_all, down_weight, contract_rows, preferred_element_type=jnp.float32)
    branch_local = gather_quarter(branch, rows)
    mixed = (widened + branch_local).astype(jnp.bfloat16)

    down_grad = blockwise_grad(up_output_all, cot_all, n_dp)
    head_grad = blockwise_grad(head_rows_all, cot_all, n_dp)
    back = jnp.concatenate(
        [
            lax.dot_general(head_flat, cot_later, contract_cols, preferred_element_type=jnp.float32),
            lax.dot_general(down_weight, cot_later, contract_cols, preferred_element_type=jnp.float32),
        ],
        axis=0,
    )
    back = lax.psum_scatter(back, "dp", scatter_dimension=1, tiled=True)
    up_upstream = (back[n_att:] * gelu_slope).astype(jnp.bfloat16)
    head_upstream = back[:n_att].astype(jnp.bfloat16).reshape(head_slice, HEADS, ROWS)
    if by_head:
        upstream = lax.all_to_all(
            head_upstream, "mp", split_axis=1, concat_axis=0, tiled=True
        ).reshape(HS, head_group * QB, TQ)
        query_grad, pair_grad = attend_back(upstream, stored)
        pair_sum = jnp.sum(
            pair_grad.reshape(HS, head_group, QB, 2, PATCHES).astype(jnp.float32), axis=2
        ).astype(jnp.bfloat16)
        grads = jnp.stack(
            [query_grad.reshape(HS, head_group, ROWS), pair_sum[:, :, 0], pair_sum[:, :, 1]]
        )
        proj_grad = lax.all_to_all(grads, "mp", split_axis=1, concat_axis=2, tiled=True)
    else:
        upstream = lax.all_to_all(
            head_upstream.reshape(head_slice, ITEMS, TQ), "mp", split_axis=1, concat_axis=0, tiled=True
        )
        query_grad, pair_grad = attend_back(upstream, stored)
        query_local, pair_local = (
            lax.all_to_all(query_grad, "mp", split_axis=0, concat_axis=1, tiled=True),
            lax.all_to_all(pair_grad, "mp", split_axis=0, concat_axis=1, tiled=True),
        )
        proj_grad = jnp.concatenate(
            [query_local.reshape(1, head_slice, HEADS, ROWS), from_items(pair_local)], axis=0
        )
    proj_grad = proj_grad.reshape(3 * head_slice * HEADS, ROWS)
    grads_all = lax.all_gather(
        jnp.concatenate([proj_grad, up_upstream], axis=0), "dp", axis=1, tiled=True
    )
    proj_grad_all, up_upstream_all = grads_all[:n_proj], grads_all[n_proj:]
    qkv_grad = blockwise_grad(proj_grad_all, hidden_all, n_dp)
    up_grad = blockwise_grad(up_upstream_all, hidden_all, n_dp)
    ratio = n_mp // n_dp
    input_pieces = jnp.concatenate(
        [
            (
                lax.dot_general(
                    proj_grad_all, qkv_flat[:, part * width:(part + 1) * width],
                    contract_rows, preferred_element_type=jnp.float32,
                )
                + lax.dot_general(
                    up_upstream_all, up_weight[:, part * width:(part + 1) * width],
                    contract_rows, preferred_element_type=jnp.float32,
                )
            ).reshape(n_dp, rows, width)
            for part in range(ratio)
        ],
        axis=0,
    )
    received = lax.all_to_all(input_pieces, "mp", split_axis=0, concat_axis=0, tiled=True)
    input_local = lax.ppermute(
        jnp.sum(received, axis=0), ("dp", "mp"), swap_by_part_pairs(n_dp, n_mp)
    )

    scaled = input_local * gain_wide
    plain_sum, cross_sum = lax.psum(
        (jnp.sum(scaled, axis=1), jnp.sum(scaled * normed, axis=1)), "mp"
    )
    tokens_grad = row_scale * (
        scaled - plain_sum[:, None] / D - normed * (cross_sum[:, None] / D)
    )
    tokens_grad = tokens_grad + cotangent.astype(jnp.float32)
    gain_piece = jnp.sum(input_local * normed, axis=0)
    gain_grad = lax.psum(gain_piece, "dp")
    return (
        mixed,
        tokens_grad,
        qkv_grad.reshape(qkv_weight.shape),
        head_grad.reshape(head_weight.shape),
        up_grad,
        down_grad,
        gain_grad,
    )


def solution(mesh):
    in_specs = (
        P("dp", "mp"),
        P("mp"),
        P(None, "mp", None, "dp"),
        P("mp", None, "dp"),
        P("mp", "dp"),
        P("mp", "dp"),
        P("dp", "mp"),
    )
    out_specs = (
        P("dp", "mp"),
        P("dp", "mp"),
        P(None, "mp", None, "dp"),
        P("mp", None, "dp"),
        P("mp", "dp"),
        P("mp", "dp"),
        P("mp"),
    )
    return jax.shard_map(shards, mesh=mesh, in_specs=in_specs, out_specs=out_specs, check_vma=False)
```

profile of v0, /device:TPU:0, one launch (start us, length us, event | category | flops | bytes accessed | tf_op | source)
XLA Modules:
  0.0 449.6 jit_solution(10410268736265085127)
XLA Ops:
  9.8 57.6 %all_to_all.75 = bf16[8,129,768]{2,1,0:T(8,128)(2,1)S(1)} all-to-all(bf16[8,129,768]{2,1,0:T(8,128)(2,1)S(1)} %broadcast_in_dim.7), channel_id=1, replica_groups=mesh['dp'=4,'mp'=8] {'mp'}, dimensions={0} | all-to-all | bytes 3170304 | tf_op jit(solution)/shard_map/all_to_all | solution.py:151
  67.3 2.4 copy.82
  69.7 2.2 reshape.250
  72.8 5.2 %all-gather.1 = f32[4,2,512]{2,1,0:T(2,128)S(1)} all-gather(f32[1,2,512]{2,1,0:T(2,128)S(1)} %maximum_bitcast_fusion), channel_id=2, replica_groups=mesh['dp'=4,'mp'=8] {'dp'}, dimensions={0}, use_global_device_ids=true | all-gather | bytes 20480 | tf_op jit(solution)/shard_map/all_gather | solution.py:206
  80.6 2.2 convolution_bitcast_fusion.2
  82.9 2.6 convolution_bitcast_fusion.1
  85.5 2.7 pad_maximum_fusion
  90.3 51.4 %all_to_all.76 = bf16[8,128,768]{1,2,0:T(8,128)(2,1)S(1)} all-to-all(bf16[8,128,768]{1,2,0:T(8,128)(2,1)S(1)} %broadcast_in_dim.6), channel_id=1, replica_groups=mesh['dp'=4,'mp'=8] {'mp'}, dimensions={0} | all-to-all | bytes 3145728 | tf_op jit(solution)/shard_map/all_to_all | solution.py:141
  141.6 2.9 copy.81
  144.5 2.8 copy.105
  147.3 2.5 convolution_bitcast_fusion.3
  149.8 4.6 %convolution_bitcast_fusion = f32[1536,512]{0,1:T(8,128)S(1)} fusion(bf16[512,1536]{1,0:T(8,128)(2,1)S(1)} %bitcast.187, bf16[1536,1536]{1,0:T(8,128)(2,1)} %param.12), kind=kOutput, calls=%fused_computation.26 | convolution fusion | flops 2415919104 | bytes 9437184 | tf_op jit(solution)/shard_map/dot_general | solution.py:275
  154.4 2.2 pad_maximum_fusion.1
  158.0 15.3 %all_to_all.77 = bf16[3,16,24,128]{3,1,0,2:T(8,128)(2,1)S(1)} all-to-all(bf16[3,16,24,128]{3,1,0,2:T(8,128)(2,1)S(1)} %copy.84), channel_id=1, replica_groups=mesh['dp'=4,'mp'=8] {'mp'}, dimensions={2} | all-to-all | bytes 589824 | tf_op jit(solution)/shard_map/all_to_all | solution.py:238
  175.2 1.8 reshape.270
  179.6 1.8 convolution_convert_fusion.17
  182.2 3.4 all-to-all-start.3
  186.4 6.5 %all-to-all-done.3 = bf16[128,3,128]{2,1,0:T(4,128)(2,1)S(1)} async-done(((bf16[128,3,128]{2,1,0:T(4,128)(2,1)}), bf16[128,3,128]{2,1,0:T(4,128)(2,1)S(1)}, u32[]{:S(2)}, u32[]{:S(2)}) %all-to-all-start.3) | async-done | bytes 98336 | tf_op jit(solution)/shard_map/all_to_all | solution.py:245
  193.2 5.4 %reduce-scatter.8.cloned.1.call-done = f32[1920,128]{0,1:T(8,128)} async-done(((f32[1920,512]{0,1:T(8,128)}), f32[1920,128]{0,1:T(8,128)}) %reduce-scatter.8.cloned.1.call-update) | async-done | bytes 983056 | tf_op jit(solution)/shard_map/reduce_scatter | solution.py:279
  200.3 5.5 %all-to-all-start.4 = ((bf16[16,24,128]{2,0,1:T(8,128)(2,1)}), bf16[16,24,128]{2,0,1:T(8,128)(2,1)S(1)}, u32[]{:S(2)}, u32[]{:S(2)}) async-start(bf16[16,24,128]{2,0,1:T(8,128)(2,1)} %copy.96), calls=%async_computation.7 | async-start | bytes 196608 | tf_op jit(solution)/shard_map/all_to_all | solution.py:283
  205.9 2.5 fusion.62
  209.3 3.7 all-to-all-done.4
  217.7 2.0 fusion.127
  220.7 3.3 bitcast_reduce_fusion
  226.2 2.2 fusion.37
  228.9 13.6 %all_to_all.78 = bf16[3,128,3,128]{3,2,0,1:T(4,128)(2,1)S(1)} all-to-all(bf16[3,128,3,128]{3,2,0,1:T(4,128)(2,1)S(1)} %copy.99), channel_id=1, replica_groups=mesh['dp'=4,'mp'=8] {'mp'}, dimensions={1} | all-to-all | bytes 589824 | tf_op jit(solution)/shard_map/all_to_all | solution.py:293
  248.1 5.1 %fusion.39 = f32[512,1536]{1,0:T(8,128)S(1)} fusion(bf16[1536,1536]{1,0:T(8,128)(2,1)} %param.12, bf16[1920,512]{0,1:T(8,128)(2,1)} %all-gather.5.cloned.1.call-done), kind=kOutput, calls=%fused_computation.70 | convolution fusion | flops 2415919104 | bytes 9437184 | tf_op jit(solution)/shard_map/dot_general | solution.py:266
  253.3 3.6 convolution_add_fusion
  256.9 5.2 %reshape.257 = f32[4,128,2,768]{3,2,1,0:T(2,128)} reshape(f32[512,1536]{1,0:T(8,128)} %convolution_add_fusion) | data formatting | bytes 6291456 | tf_op jit(solution)/shard_map/reshape | solution.py:160
  262.1 3.9 copy.93
  268.3 3.6 convolution_convert_fusion.6
  272.0 1.9 fusion.18
  273.9 3.6 convolution_convert_fusion.5
  277.5 3.7 fusion.20
  281.2 3.2 fusion.22
  286.8 1.9 pad_maximum_fusion.2
  288.7 4.8 %all-to-all-start.6 = ((f32[8,128,768]{2,1,0:T(8,128)}), f32[8,128,768]{2,1,0:T(8,128)}, u32[]{:S(2)}, u32[]{:S(2)}) async-start(f32[8,128,768]{2,1,0:T(8,128)} %pad_maximum_fusion.2), calls=%async_computation.9 | async-start | bytes 6291456 | tf_op jit(solution)/shard_map/all_to_all | solution.py:330
  299.6 3.9 add_convert_fusion
  309.9 4.0 fusion.5
  314.0 3.9 add_convert_fusion.1
  317.8 59.0 %all-to-all-done.6 = f32[8,128,768]{2,1,0:T(8,128)} async-done(((f32[8,128,768]{2,1,0:T(8,128)}), f32[8,128,768]{2,1,0:T(8,128)}, u32[]{:S(2)}, u32[]{:S(2)}) %all-to-all-start.6) | async-done | bytes 3145760 | tf_op jit(solution)/shard_map/all_to_all | solution.py:330
  376.9 2.8 reduce_sum.199
  379.7 1.9 collective-permute-start.3
  381.6 6.1 %fusion.3 = bf16[1152,1536]{1,0:T(8,128)(2,1)} fusion(f32[1152,1536]{1,0:T(8,128)} %fusion.5, bf16[512,1536]{1,0:T(8,128)(2,1)S(1)} %copy-done.3, bf16[2688,512]{0,1:T(8,128)(2,1)} %all-gather.7.cloned.1.call-done), kind=kOutput, calls=%fused_computation.6 | convolution fusion | flops 460062720 | bytes 11304960 | tf_op jit(solution)/shard_map/dot_general | solution.py:180
  387.7 24.3 %reduce-scatter.6.cloned.1.call-done = f32[1,128,768]{2,1,0:T(8,128)} async-done(((f32[8,128,768]{2,1,0:T(8,128)}), f32[1,128,768]{2,1,0:T(8,128)}) %reduce-scatter.6.cloned.1.call-update) | async-done | bytes 393232 | tf_op jit(solution)/shard_map/reduce_scatter | solution.py:162
  412.0 1.6 collective-permute-start.2
  413.9 7.1 %psum.23 = f32[768]{0:T(1024)} all-reduce(f32[768]{0:T(1024)S(1)} %get-tuple-element.13), channel_id=1, replica_groups=mesh['dp'=4,'mp'=8] {'dp'}, use_global_device_ids=true, to_apply=%region_25.0 | all-reduce | flops 768 | bytes 6144 | tf_op jit(solution)/shard_map/psum | solution.py:344
  421.0 20.6 %all-reduce = (f32[128]{0:T(128)S(1)}, f32[128]{0:T(128)S(1)}) all-reduce(f32[128]{0:T(128)S(1)} %get-tuple-element.14, f32[128]{0:T(128)S(1)} %get-tuple-element.15), channel_id=1, replica_groups=mesh['dp'=4,'mp'=8] {'mp'}, use_global_device_ids=true, to_apply=%region_23.0 | all-reduce | flops 256 | bytes 2048 | tf_op jit(solution)/shard_map/psum | solution.py:336
  (185 shorter events, 50.7 us)
Async XLA Ops:
  7.2 140.1 %copy-start = (bf16[16,24,1536]{2,1,0:T(8,128)(2,1)S(1)}, bf16[16,24,1536]{2,1,0:T(8,128)(2,1)}, u32[]{:S(2)}) copy-start(bf16[16,24,1536]{2,1,0:T(8,128)(2,1)} %param.10) | copy-start | bytes 3538948
  7.2 140.1 %reduce-scatter.4.cloned.1.call-start = ((), (), s32[]{:S(2)}) async-start(), calls=%async_computation.10 | async-start | bytes 6881280 | tf_op jit(solution)/shard_map/reduce_scatter | solution.py:228
  8.9 0.7 collective-permute-start.1
  78.0 1.2 copy-start.30
  78.1 2.6 copy-start.32
  78.6 4.2 copy-start.2
  78.6 4.2 slice-start.4
  80.6 2.2 slice-start.5
  88.3 110.3 %reduce-scatter.8.cloned.1.call-start = ((), (), s32[]{:S(2)}) async-start(), calls=%async_computation.13 | async-start | bytes 4915200 | tf_op jit(solution)/shard_map/reduce_scatter | solution.py:279
  89.2 0.7 collective-permute-start
  147.3 2.5 copy-start.15
  173.4 4.5 %copy-start.25 = (f32[24,16]{1,0:T(8,128)}, f32[24,16]{1,0:T(8,128)S(1)}, u32[]{:S(2)}) copy-start(f32[24,16]{1,0:T(8,128)S(1)} %div.67) | copy-start | bytes 4612
  173.5 4.4 copy-start.27
  177.1 2.5 copy-start.17
  177.5 1.1 copy-start.4
  179.6 13.4 %copy-start.29 = (f32[24,16,128]{2,1,0:T(8,128)}, f32[24,16,128]{2,1,0:T(8,128)S(1)}, u32[]{:S(2)}) copy-start(f32[24,16,128]{2,1,0:T(8,128)S(1)} %fusion.52) | copy-start | bytes 589828
  182.2 10.7 %all-to-all-start.3 = ((bf16[128,3,128]{2,1,0:T(4,128)(2,1)}), bf16[128,3,128]{2,1,0:T(4,128)(2,1)S(1)}, u32[]{:S(2)}, u32[]{:S(2)}) async-start(bf16[128,3,128]{2,1,0:T(4,128)(2,1)} %copy.89), calls=%async_computation.4 | async-start | bytes 262144 | tf_op jit(solution)/shard_map/all_to_all | solution.py:245
  200.3 12.6 %all-to-all-start.4 = ((bf16[16,24,128]{2,0,1:T(8,128)(2,1)}), bf16[16,24,128]{2,0,1:T(8,128)(2,1)S(1)}, u32[]{:S(2)}, u32[]{:S(2)}) async-start(bf16[16,24,128]{2,0,1:T(8,128)(2,1)} %copy.96), calls=%async_computation.7 | async-start | bytes 196608 | tf_op jit(solution)/shard_map/all_to_all | solution.py:283
  205.8 42.3 %all-gather.5.cloned.1.call-start = ((), (), s32[]{:S(2)}) async-start(), calls=%async_computation.11 | async-start | bytes 2457600 | tf_op jit(solution)/shard_map/all_gather | solution.py:260
  209.2 68.3 %all-gather.7.cloned.1.call-start = ((), (), s32[]{:S(2)}) async-start(), calls=%async_computation.14 | async-start | bytes 3440640 | tf_op jit(solution)/shard_map/all_gather | solution.py:307
  216.1 3.6 copy-start.18
  216.1 3.6 copy-start.26
  216.1 3.6 copy-start.28
  216.1 4.6 %copy-start.24 = (f32[24,128]{1,0:T(8,128)S(1)}, f32[24,128]{1,0:T(8,128)}, u32[]{:S(2)}) copy-start(f32[24,128]{1,0:T(8,128)} %copy-done.23) | copy-start | bytes 36868
  226.2 2.5 copy-start.19
  228.6 16.3 %copy-start.16 = (bf16[1536,128]{0,1:T(8,128)(2,1)S(1)}, bf16[1536,128]{0,1:T(8,128)(2,1)}, u32[]{:S(2)}) copy-start(bf16[1536,128]{0,1:T(8,128)(2,1)} %get-tuple-element.26) | copy-start | bytes 1179652
  242.5 3.6 copy-start.31
  245.9 166.1 %reduce-scatter.6.cloned.1.call-start = ((), (), s32[]{:S(2)}) async-start(), calls=%async_computation.12 | async-start | bytes 3538944 | tf_op jit(solution)/shard_map/reduce_scatter | solution.py:162
  266.0 2.4 copy-start.6
  268.3 3.6 copy-start.11
  277.5 3.7 copy-start.8
  281.2 3.2 copy-start.33
  288.7 4.8 %copy-start.10 = (bf16[1,128,2,768]{1,3,2,0:T(8,128)(2,1)S(1)}, bf16[1,128,2,768]{1,3,2,0:T(8,128)(2,1)}, u32[]{:S(2)}) copy-start(bf16[1,128,2,768]{1,3,2,0:T(8,128)(2,1)} %get-tuple-element.23) | copy-start | bytes 1179652
  288.7 88.2 %all-to-all-start.6 = ((f32[8,128,768]{2,1,0:T(8,128)}), f32[8,128,768]{2,1,0:T(8,128)}, u32[]{:S(2)}, u32[]{:S(2)}) async-start(f32[8,128,768]{2,1,0:T(8,128)} %pad_maximum_fusion.2), calls=%async_computation.9 | async-start | bytes 6291456 | tf_op jit(solution)/shard_map/all_to_all | solution.py:330
  293.5 1.6 copy-start.7
  293.6 5.3 %slice-start.2 = ((s8[4718592]{0:T(1024)(128)(4,1)}), s8[4194304]{0:T(1024)(128)(4,1)S(1)}, s32[]{:S(2)}) async-start(s8[4718592]{0:T(1024)(128)(4,1)} %bitcast.156), calls=%async_computation.17 | async-start | bytes 8388608
  295.1 2.1 copy-start.5
  295.1 2.1 copy-start.13
  295.1 3.7 slice-start.3
  296.6 2.6 slice-start
  297.3 2.3 slice-start.1
  299.6 3.9 copy-start.3
  299.6 3.9 copy-start.9
  379.7 33.9 %copy-start.14 = (bf16[128,768]{1,0:T(8,128)(2,1)S(1)}, bf16[128,768]{1,0:T(8,128)(2,1)}, u32[]{:S(2)}) copy-start(bf16[128,768]{1,0:T(8,128)(2,1)} %param.7) | copy-start | bytes 589828
  379.7 61.9 %copy-start.22 = (bf16[128,768]{1,0:T(8,128)(2,1)S(1)}, bf16[128,768]{1,0:T(8,128)(2,1)}, u32[]{:S(2)}) copy-start(bf16[128,768]{1,0:T(8,128)(2,1)} %param.13) | copy-start | bytes 589828
  379.7 33.9 %collective-permute-start.3 = (f32[128,768]{1,0:T(8,128)}, f32[128,768]{1,0:T(8,128)S(1)}, u32[]{:S(2)}, u32[]{:S(2)}) collective-permute-start(f32[128,768]{1,0:T(8,128)} %reduce_sum.199), channel_id=1, source_target_pairs={{0,0},{1,8},{2,16},{3,24},{4,1},{5,9},{6,17},{7,25},{8,2},{9,10},{... | collective-permute-start | bytes 1179656 | tf_op jit(solution)/shard_map/ppermute | solution.py:331
  381.6 61.0 %copy-start.1 = (bf16[16,24,1536]{2,1,0:T(8,128)(2,1)S(1)}, bf16[16,24,1536]{2,1,0:T(8,128)(2,1)}, u32[]{:S(2)}) copy-start(bf16[16,24,1536]{2,1,0:T(8,128)(2,1)} %param.10) | copy-start | bytes 3538948
  412.0 29.6 %collective-permute-start.2 = (f32[128,768]{1,0:T(8,128)}, f32[128,768]{1,0:T(8,128)S(1)}, u32[]{:S(2)}, u32[]{:S(2)}) collective-permute-start(f32[128,768]{1,0:T(8,128)} %bitcast.209), channel_id=1, source_target_pairs={{0,0},{1,1},{2,8},{3,9},{4,16},{5,17},{6,24},{7,25},{8,2},{9,3},{1... | collective-permute-start | bytes 1179656 | tf_op jit(solution)/shard_map/ppermute | solution.py:133
  (4 other events, 3.2 us)
Sparse Core Ops, SparseCore 0:
  88.4 51.7 reduce-scatter.3
  156.7 41.8 reduce-scatter.7
  209.3 22.2 all-gather.4
  246.0 24.0 all-gather.6
  273.5 138.4 reduce-scatter.5
where the time goes:
time: 458 us; the launch traced here: 450 us
  blocking collectives  171 us (37%)
  waiting for transfers between devices  99 us (22%)
  matrix products  79.7 us (17%)
  local copies, waits for them, and re-layouts  43.4 us (9%)
  other arithmetic  22.7 us (5%)
  starting transfers between devices  19 us (4%)
  between operations  15 us (3%)
    all_to_all x1, waiting for transfers between devices, shards(): lax.all_to_all(input_pieces, 'mp', split_axis=0, concat_axis=0, tiled=True)  59 us
    all_to_all x1, blocking collectives, spread_quarter_rows(): lax.all_to_all(copies, 'mp', split_axis=0, concat_axis=0, tiled=True)  57.6 us
    all_to_all x1, blocking collectives, spread_quarter(): lax.all_to_all(copies, 'mp', split_axis=0, concat_axis=0, tiled=True)  51.4 us
    dot_general x16, matrix products, blockwise_grad(): jnp.dot(left[:, block * rows:(block + 1) * rows], right[block * rows:(blo...  39.3 us
    reduce_scatter x1, waiting for transfers between devices, gather_quarter(): summed = lax.psum_scatter(pieces, 'mp', scatter_dimension=0, tiled=True)  24.3 us
    psum x1, blocking collectives, shards(): lax.psum((jnp.sum(scaled, axis=1), jnp.sum(scaled * normed, axis=1)), 'mp')  20.6 us
    all_to_all x1, blocking collectives, shards(): lax.all_to_all(projected, 'mp', split_axis=2, concat_axis=1, tiled=True)  15.3 us
    all_to_all x1, blocking collectives, shards(): lax.all_to_all(grads, 'mp', split_axis=1, concat_axis=2, tiled=True)  13.6 us
  transfers between devices with their start and end apart: 12, of which 5 were waited for; matrix products, arithmetic and copies ran while one was open for 25% of the time, Pallas kernels for 0%

commit v1 on v0

--- a/solution.py
+++ b/solution.py
@@ -261,10 +261,26 @@
         jnp.concatenate([head_rows, up_output], axis=0), "dp", axis=1, tiled=True
     )
     head_rows_all, up_output_all = both_all[:n_att], both_all[n_att:]
-    branch = lax.dot_general(
-        head_rows_all, head_flat, contract_rows, preferred_element_type=jnp.float32
-    ) + lax.dot_general(up_output_all, down_weight, contract_rows, preferred_element_type=jnp.float32)
-    branch_local = gather_quarter(branch, rows)
+    branch_pieces = jnp.concatenate(
+        [
+            (
+                lax.dot_general(
+                    head_rows_all, head_flat[:, part * width:(part + 1) * width],
+                    contract_rows, preferred_element_type=jnp.float32,
+                )
+                + lax.dot_general(
+                    up_output_all, down_weight[:, part * width:(part + 1) * width],
+                    contract_rows, preferred_element_type=jnp.float32,
+                )
+            ).reshape(n_dp, rows, width)
+            for part in range(n_mp // n_dp)
+        ],
+        axis=0,
+    )
+    branch_summed = lax.psum_scatter(branch_pieces, "mp", scatter_dimension=0, tiled=True)
+    branch_local = lax.ppermute(
+        branch_summed.reshape(rows, width), ("dp", "mp"), swap_by_part_pairs(n_dp, n_mp)
+    )
     mixed = (widened + branch_local).astype(jnp.bfloat16)
 
     down_grad = blockwise_grad(up_output_all, cot_all, n_dp)

time: 458 us -> 467 us (1.020)
  matrix products: 79.7 us -> 89.7 us
  other arithmetic: 22.7 us -> 28.2 us
    dot_general x16, matrix products: 39.3 us -> 45.9 us  [blockwise_grad(): jnp.dot(left[:, block * rows:(block + 1) * rows], right[block * rows:(blo...]
    reduce_scatter x1, waiting for transfers between devices: 5.42 us -> 0.01 us  [shards(): back = lax.psum_scatter(back, 'dp', scatter_dimension=1, tiled=True)]
    reshape x1 -> x0, local copies, waits for them, and re-layouts: 5.15 us -> none  [gather_quarter(): pieces = partial.reshape(n_dp, rows, ratio, width)]
    unnamed x81 -> x67, local copies, waits for them, and re-layouts: 9.69 us -> 6.99 us
  transfers between devices with their start and end apart: 12 -> 12, of which waited for: 5 -> 4; matrix products, arithmetic and copies ran while one was open for 25% -> 28% of each run, Pallas kernels for 0% -> 0%
where the time goes in v1:
time: 467 us; the launch traced here: 458 us
  blocking collectives  170 us (36%)
  waiting for transfers between devices  99.6 us (21%)
  matrix products  89.7 us (19%)
  local copies, waits for them, and re-layouts  38.8 us (8%)
  other arithmetic  28.2 us (6%)
  starting transfers between devices  16.8 us (4%)
  between operations  15 us (3%)
    all_to_all x1, waiting for transfers between devices, shards(): lax.all_to_all(input_pieces, 'mp', split_axis=0, concat_axis=0, tiled=True)  61.4 us
    all_to_all x1, blocking collectives, spread_quarter_rows(): lax.all_to_all(copies, 'mp', split_axis=0, concat_axis=0, tiled=True)  57.6 us
    all_to_all x1, blocking collectives, spread_quarter(): lax.all_to_all(copies, 'mp', split_axis=0, concat_axis=0, tiled=True)  51.3 us
    dot_general x16, matrix products, blockwise_grad(): jnp.dot(left[:, block * rows:(block + 1) * rows], right[block * rows:(blo...  45.9 us
    reduce_scatter x1, waiting for transfers between devices, shards(): lax.psum_scatter(branch_pieces, 'mp', scatter_dimension=0, tiled=True)  29 us
    psum x1, blocking collectives, shards(): lax.psum((jnp.sum(scaled, axis=1), jnp.sum(scaled * normed, axis=1)), 'mp')  22 us
    all_to_all x1, blocking collectives, shards(): lax.all_to_all(projected, 'mp', split_axis=2, concat_axis=1, tiled=True)  15.3 us
    all_to_all x1, blocking collectives, shards(): lax.all_to_all(grads, 'mp', split_axis=1, concat_axis=2, tiled=True)  12.1 us
  transfers between devices with their start and end apart: 12, of which 4 were waited for; matrix products, arithmetic and copies ran while one was open for 28% of the time, Pallas kernels for 0%

profile of v1, /device:TPU:0, one launch (start us, length us, event | category | flops | bytes accessed | tf_op | source)
XLA Modules:
  0.0 458.4 jit_solution(2318867357250496725)
XLA Ops:
  9.7 57.6 %all_to_all.75 = bf16[8,129,768]{2,1,0:T(8,128)(2,1)S(1)} all-to-all(bf16[8,129,768]{2,1,0:T(8,128)(2,1)S(1)} %broadcast_in_dim.7), channel_id=1, replica_groups=mesh['dp'=4,'mp'=8] {'mp'}, dimensions={0} | all-to-all | bytes 3170304 | tf_op jit(solution)/shard_map/all_to_all | solution.py:151
  70.4 5.2 %all-gather.1 = f32[4,2,512]{2,1,0:T(2,128)S(1)} all-gather(f32[1,2,512]{2,1,0:T(2,128)S(1)} %maximum_bitcast_fusion), channel_id=2, replica_groups=mesh['dp'=4,'mp'=8] {'dp'}, dimensions={0}, use_global_device_ids=true | all-gather | bytes 20480 | tf_op jit(solution)/shard_map/all_gather | solution.py:206
  77.7 2.2 convolution_bitcast_fusion.2
  80.0 2.6 convolution_bitcast_fusion.1
  82.6 2.7 pad_maximum_fusion
  87.3 51.3 %all_to_all.76 = bf16[8,128,768]{1,2,0:T(8,128)(2,1)S(1)} all-to-all(bf16[8,128,768]{1,2,0:T(8,128)(2,1)S(1)} %broadcast_in_dim.6), channel_id=1, replica_groups=mesh['dp'=4,'mp'=8] {'mp'}, dimensions={0} | all-to-all | bytes 3145728 | tf_op jit(solution)/shard_map/all_to_all | solution.py:141
  138.7 2.9 copy.77
  141.6 2.8 copy.100
  144.4 2.9 convolution_bitcast_fusion.3
  147.2 4.6 convolution_bitcast_fusion
  151.8 2.2 pad_maximum_fusion.1
  157.0 15.3 %all_to_all.77 = bf16[3,16,24,128]{3,1,0,2:T(8,128)(2,1)S(1)} all-to-all(bf16[3,16,24,128]{3,1,0,2:T(8,128)(2,1)S(1)} %copy.80), channel_id=1, replica_groups=mesh['dp'=4,'mp'=8] {'mp'}, dimensions={2} | all-to-all | bytes 589824 | tf_op jit(solution)/shard_map/all_to_all | solution.py:238
  174.5 2.5 copy.84
  184.8 4.0 all-to-all-start.3
  190.6 5.5 %all-to-all-done.3 = bf16[128,3,128]{2,1,0:T(4,128)(2,1)} async-done(((bf16[128,3,128]{2,1,0:T(4,128)(2,1)}), bf16[128,3,128]{2,1,0:T(4,128)(2,1)}, u32[]{:S(2)}, u32[]{:S(2)}) %all-to-all-start.3) | async-done | bytes 98336 | tf_op jit(solution)/shard_map/all_to_all | solution.py:245
  201.3 3.4 all-to-all-start.4
  204.7 2.5 fusion.66
  208.1 3.6 all-to-all-done.4
  214.7 2.2 fusion.67
  216.9 2.7 fusion.134
  222.4 4.1 bitcast_reduce_fusion
  227.2 2.4 convolution_convert_fusion.16
  229.6 2.2 fusion.41
  232.4 12.1 %all_to_all.78 = bf16[3,128,3,128]{3,2,0,1:T(4,128)(2,1)S(1)} all-to-all(bf16[3,128,3,128]{3,2,0,1:T(4,128)(2,1)S(1)} %copy.94), channel_id=1, replica_groups=mesh['dp'=4,'mp'=8] {'mp'}, dimensions={1} | all-to-all | bytes 589824 | tf_op jit(solution)/shard_map/all_to_all | solution.py:309
  245.6 1.9 reshape.262
  248.7 1.9 pad_maximum_fusion.4
  252.9 3.8 fusion.24
  257.3 3.1 fusion.26
  260.9 1.9 pad_maximum_fusion.2
  263.9 2.8 fusion.17
  266.7 3.6 convolution_convert_fusion.6
  270.3 1.9 fusion.18
  272.2 3.6 convolution_convert_fusion.5
  275.8 3.7 fusion.20
  279.5 3.2 fusion.22
  285.1 1.9 pad_maximum_fusion.3
  287.0 5.3 %all-to-all-start.6 = ((f32[8,128,768]{2,1,0:T(8,128)}), f32[8,128,768]{2,1,0:T(8,128)}, u32[]{:S(2)}, u32[]{:S(2)}) async-start(f32[8,128,768]{2,1,0:T(8,128)} %pad_maximum_fusion.3), calls=%async_computation.9 | async-start | bytes 6291456 | tf_op jit(solution)/shard_map/all_to_all | solution.py:346
  293.9 3.8 convolution_convert_fusion.4
  297.7 3.3 fusion.16
  301.1 5.0 %add_convert_fusion = bf16[1536,1536]{1,0:T(8,128)(2,1)} fusion(bf16[1536,1536]{1,0:T(8,128)(2,1)S(1)} %convolution_convert_fusion.4, bf16[1536,1536]{1,0:T(8,128)(2,1)S(1)} %bitcast.153, bf16[1536,1536]{1,0:T(8,128)(2,1)S(1)} %bitcast.151, bf16[128,1536]{0,1:T(8,128)(2,1)S(1)} %bitcast.175, bf16[1920,512]{0,1:T(8,128)(2,1)} %all-gather.5.cloned.1.call-done), kind=kOutput, calls=%fused_computation.1 | convolution fusion | flops 625213440 | bytes 19660800 | tf_op jit(solution)/shard_map/dot_general | solution.py:180
  312.6 4.0 fusion.5
  316.6 3.9 add_convert_fusion.1
  320.4 61.4 %all-to-all-done.6 = f32[8,128,768]{2,1,0:T(8,128)} async-done(((f32[8,128,768]{2,1,0:T(8,128)}), f32[8,128,768]{2,1,0:T(8,128)}, u32[]{:S(2)}, u32[]{:S(2)}) %all-to-all-start.6) | async-done | bytes 3145760 | tf_op jit(solution)/shard_map/all_to_all | solution.py:346
  381.9 2.1 reduce_sum.199
  384.8 6.0 %fusion.3 = bf16[1152,1536]{1,0:T(8,128)(2,1)} fusion(f32[1152,1536]{1,0:T(8,128)} %fusion.5, bf16[512,1536]{1,0:T(8,128)(2,1)S(1)} %fusion.11, bf16[2688,512]{0,1:T(8,128)(2,1)} %all-gather.7.cloned.1.call-done), kind=kOutput, calls=%fused_computation.6 | convolution fusion | flops 460062720 | bytes 11304960 | tf_op jit(solution)/shard_map/dot_general | solution.py:180
  390.8 29.0 %reduce-scatter.6.cloned.1.call-done = f32[1,128,768]{2,1,0:T(8,128)} async-done(((f32[8,128,768]{2,1,0:T(8,128)}), f32[1,128,768]{2,1,0:T(8,128)}) %reduce-scatter.6.cloned.1.call-update) | async-done | bytes 393232 | tf_op jit(solution)/shard_map/reduce_scatter | solution.py:280
  421.7 6.8 %psum.23 = f32[768]{0:T(1024)} all-reduce(f32[768]{0:T(1024)S(1)} %get-tuple-element.13), channel_id=1, replica_groups=mesh['dp'=4,'mp'=8] {'dp'}, use_global_device_ids=true, to_apply=%region_25.0 | all-reduce | flops 768 | bytes 6144 | tf_op jit(solution)/shard_map/psum | solution.py:360
  428.5 22.0 %all-reduce = (f32[128]{0:T(128)S(1)}, f32[128]{0:T(128)S(1)}) all-reduce(f32[128]{0:T(128)S(1)} %get-tuple-element.14, f32[128]{0:T(128)S(1)} %get-tuple-element.15), channel_id=1, replica_groups=mesh['dp'=4,'mp'=8] {'mp'}, use_global_device_ids=true, to_apply=%region_23.0 | all-reduce | flops 256 | bytes 2048 | tf_op jit(solution)/shard_map/psum | solution.py:352
  (172 shorter events, 58.1 us)
Async XLA Ops:
  7.2 137.2 %reduce-scatter.4.cloned.1.call-start = ((), (), s32[]{:S(2)}) async-start(), calls=%async_computation.10 | async-start | bytes 6881280 | tf_op jit(solution)/shard_map/reduce_scatter | solution.py:228
  8.8 0.7 collective-permute-start.1
  75.7 1.2 copy-start.23
  75.7 2.0 copy-start.25
  76.3 3.7 slice-start.4
  77.7 2.2 slice-start.5
  85.4 0.9 copy-start.15
  85.4 114.2 %reduce-scatter.8.cloned.1.call-start = ((), (), s32[]{:S(2)}) async-start(), calls=%async_computation.13 | async-start | bytes 4915200 | tf_op jit(solution)/shard_map/reduce_scatter | solution.py:295
  86.3 0.7 collective-permute-start
  144.4 2.9 copy-start.12
  178.9 2.2 copy-start.19
  178.9 2.2 copy-start.21
  179.3 1.1 copy-start
  180.5 0.6 copy-start.17
  184.8 11.4 %all-to-all-start.3 = ((bf16[128,3,128]{2,1,0:T(4,128)(2,1)}), bf16[128,3,128]{2,1,0:T(4,128)(2,1)}, u32[]{:S(2)}, u32[]{:S(2)}) async-start(bf16[128,3,128]{2,1,0:T(4,128)(2,1)} %copy.85), calls=%async_computation.4 | async-start | bytes 262144 | tf_op jit(solution)/shard_map/all_to_all | solution.py:245
  200.6 6.6 %copy-start.14 = (bf16[384,128]{0,1:T(8,128)(2,1)S(1)}, bf16[384,128]{0,1:T(8,128)(2,1)}, u32[]{:S(2)}) copy-start(bf16[384,128]{0,1:T(8,128)(2,1)} %copy.88) | copy-start | bytes 294916
  201.3 10.4 %all-to-all-start.4 = ((bf16[16,24,128]{2,0,1:T(8,128)(2,1)}), bf16[16,24,128]{2,0,1:T(8,128)(2,1)S(1)}, u32[]{:S(2)}, u32[]{:S(2)}) async-start(bf16[16,24,128]{2,0,1:T(8,128)(2,1)} %copy.91), calls=%async_computation.7 | async-start | bytes 196608 | tf_op jit(solution)/shard_map/all_to_all | solution.py:299
  204.6 48.2 %all-gather.5.cloned.1.call-start = ((), (), s32[]{:S(2)}) async-start(), calls=%async_computation.11 | async-start | bytes 2457600 | tf_op jit(solution)/shard_map/all_gather | solution.py:260
  208.0 8.9 %copy-start.18 = (f32[24,128]{1,0:T(8,128)S(1)}, f32[24,128]{1,0:T(8,128)}, u32[]{:S(2)}) copy-start(f32[24,128]{1,0:T(8,128)} %copy-done.17) | copy-start | bytes 36868
  208.0 8.9 %copy-start.20 = (f32[24,16]{1,0:T(8,128)S(1)}, f32[24,16]{1,0:T(8,128)}, u32[]{:S(2)}) copy-start(f32[24,16]{1,0:T(8,128)} %div.67) | copy-start | bytes 4612
  208.0 8.9 %copy-start.22 = (f32[24,16]{1,0:T(8,128)S(1)}, f32[24,16]{1,0:T(8,128)}, u32[]{:S(2)}) copy-start(f32[24,16]{1,0:T(8,128)} %rsqrt.32) | copy-start | bytes 4612
  208.0 67.8 %all-gather.7.cloned.1.call-start = ((), (), s32[]{:S(2)}) async-start(), calls=%async_computation.14 | async-start | bytes 3440640 | tf_op jit(solution)/shard_map/all_gather | solution.py:323
  229.6 2.2 copy-start.10
  244.6 6.3 %copy-start.24 = (bf16[768]{0:T(1024)(128)(2,1)S(1)}, bf16[768]{0:T(1024)(128)(2,1)}, u32[]{:S(2)}) copy-start(bf16[768]{0:T(1024)(128)(2,1)} %param.8) | copy-start | bytes 4612
  250.6 169.2 %reduce-scatter.6.cloned.1.call-start = ((), (), s32[]{:S(2)}) async-start(), calls=%async_computation.12 | async-start | bytes 3538944 | tf_op jit(solution)/shard_map/reduce_scatter | solution.py:280
  252.9 3.8 copy-start.13
  252.9 3.8 copy-start.2
  262.9 1.0 copy-start.8
  262.9 3.8 copy-start.3
  266.7 3.6 copy-start.7
  275.8 3.7 copy-start.4
  279.5 3.2 copy-start.26
  287.0 5.3 %copy-start.6 = (bf16[1,128,2,768]{1,3,2,0:T(8,128)(2,1)S(1)}, bf16[1,128,2,768]{1,3,2,0:T(8,128)(2,1)}, u32[]{:S(2)}) copy-start(bf16[1,128,2,768]{1,3,2,0:T(8,128)(2,1)} %get-tuple-element.23) | copy-start | bytes 1179652
  287.0 94.9 %all-to-all-start.6 = ((f32[8,128,768]{2,1,0:T(8,128)}), f32[8,128,768]{2,1,0:T(8,128)}, u32[]{:S(2)}, u32[]{:S(2)}) async-start(f32[8,128,768]{2,1,0:T(8,128)} %pad_maximum_fusion.3), calls=%async_computation.9 | async-start | bytes 6291456 | tf_op jit(solution)/shard_map/all_to_all | solution.py:346
  292.3 8.7 %slice-start = ((s8[4718592]{0:T(1024)(128)(4,1)}), s8[4194304]{0:T(1024)(128)(4,1)S(1)}, s32[]{:S(2)}) async-start(s8[4718592]{0:T(1024)(128)(4,1)} %bitcast.150), calls=%async_computation.15 | async-start | bytes 8388608
  292.3 8.7 %slice-start.2 = ((s8[4718592]{0:T(1024)(128)(4,1)}), s8[4194304]{0:T(1024)(128)(4,1)S(1)}, s32[]{:S(2)}) async-start(s8[4718592]{0:T(1024)(128)(4,1)} %bitcast.152), calls=%async_computation.17 | async-start | bytes 8388608
  293.9 3.9 copy-start.1
  293.9 3.9 copy-start.9
  293.9 7.1 %slice-start.1 = ((s8[4718592]{0:T(1024)(128)(4,1)}), s8[524288]{0:T(1024)(128)(4,1)S(1)}, s32[]{:S(2)}) async-start(s8[4718592]{0:T(1024)(128)(4,1)} %bitcast.150), calls=%async_computation.16 | async-start | bytes 1048576
  293.9 7.1 %slice-start.3 = ((s8[4718592]{0:T(1024)(128)(4,1)}), s8[524288]{0:T(1024)(128)(4,1)S(1)}, s32[]{:S(2)}) async-start(s8[4718592]{0:T(1024)(128)(4,1)} %bitcast.152), calls=%async_computation.18 | async-start | bytes 1048576
  301.0 5.1 %copy-start.5 = (bf16[2688,512]{0,1:T(8,128)(2,1)S(1)}, bf16[2688,512]{0,1:T(8,128)(2,1)}, u32[]{:S(2)}) copy-start(bf16[2688,512]{0,1:T(8,128)(2,1)} %all-gather.7.cloned.1.call-done) | copy-start | bytes 8257540
  384.0 37.5 %copy-start.11 = (bf16[128,768]{1,0:T(8,128)(2,1)S(1)}, bf16[128,768]{1,0:T(8,128)(2,1)}, u32[]{:S(2)}) copy-start(bf16[128,768]{1,0:T(8,128)(2,1)} %param.7) | copy-start | bytes 589828
  384.0 66.5 %copy-start.16 = (bf16[128,768]{1,0:T(8,128)(2,1)S(1)}, bf16[128,768]{1,0:T(8,128)(2,1)}, u32[]{:S(2)}) copy-start(bf16[128,768]{1,0:T(8,128)(2,1)} %param.13) | copy-start | bytes 589828
  384.0 37.5 %collective-permute-start.3 = (f32[128,768]{1,0:T(8,128)S(1)}, f32[128,768]{1,0:T(8,128)S(1)}, u32[]{:S(2)}, u32[]{:S(2)}) collective-permute-start(f32[128,768]{1,0:T(8,128)S(1)} %reduce_sum.199), channel_id=1, source_target_pairs={{0,0},{1,8},{2,16},{3,24},{4,1},{5,9},{6,17},{7,25},{8,2},{9,10},{... | collective-permute-start | bytes 1179656 | tf_op jit(solution)/shard_map/ppermute | solution.py:347
  419.8 30.7 %collective-permute-start.2 = (f32[128,768]{1,0:T(8,128)}, f32[128,768]{1,0:T(8,128)S(1)}, u32[]{:S(2)}, u32[]{:S(2)}) collective-permute-start(f32[128,768]{1,0:T(8,128)} %bitcast.208), channel_id=1, source_target_pairs={{0,0},{1,8},{2,16},{3,24},{4,1},{5,9},{6,17},{7,25},{8,2},{9,10},{... | collective-permute-start | bytes 1179656 | tf_op jit(solution)/shard_map/ppermute | solution.py:281
Sparse Core Ops, SparseCore 0:
  85.5 51.7 reduce-scatter.3
  154.1 41.7 reduce-scatter.7
  208.1 22.2 all-gather.4
  250.7 24.3 all-gather.6
  278.5 141.2 reduce-scatter.5
